TPU v7x, 512 devices: a whole 4x8x8 slice. The times are simulated.
512 devices in a mesh: lat: 64 (over y, x, core), row: 8 (over z).
Axes of the slice: x: 4, y: 8, z: 8, core: 2. Of those that a mesh axis runs over, the one named last changes fastest.
Arguments:
- activations: float32 [12288, 8192], P('lat', 'row'), may hold values from -15 to 15
- center_bias: float32 [8192], P('row'), may hold values from -3 to 3
- encoder_weight: bfloat16 [8192, 16384], P('row', 'lat'), may hold values from -0.0625 to 0.0625
- encoder_bias: float32 [16384], P('lat'), may hold values from -3 to 3
- decoder_weight: bfloat16 [16384, 8192], P('lat', 'row'), may hold values from -1 to 1
- row_blocks: int32 [12288, 4], P('lat'), may hold values from 0 to 127, all different within a row; in each aligned block of 192 rows (0 to 191, 192 to 383, ...) at most 12 rows name the same one
- pick_offsets: int32 [12288, 4, 8], P('lat'), may hold values from 0 to 127
Outputs:
- encoder_grad: bfloat16 [8192, 16384], P('row', 'lat')
- decoder_grad: bfloat16 [16384, 8192], P('lat', 'row')
- bias_grad: float32 [16384], P('lat')
- row_loss: float32 [12288], P('lat')
Inputs may be any that keep to these rules, and one draw needn't show every extreme that they name: `row_blocks`: the 4 blocks of a row differ. Within each group of 192 rows (the rows of one lat index), at most 12 rows name the same block, and in some groups one block is named by exactly 12 rows.
All inputs are finite; a program needn't handle non-finite values.
Results may differ from a plain program's by a relative error of at most 0.006.
Values may be sent and summed in bfloat16 or wider, within the bound.
No kernel may reach another device: no remote copies, remote signals or barrier semaphores. Data moves between devices by JAX's collectives and lax.ppermute only.
A program may use at most 64 MiB of HBM per device.

v0:
```python
import jax
import jax.numpy as jnp
from jax import lax
from jax.sharding import PartitionSpec as P

D = 8192
BLK = 128
KB = 4
PER = 8


def slot_targets(row_blocks, total_blocks, capacity):
    pair_blocks = row_blocks.reshape(-1)
    onehot = (pair_blocks[:, None] == jnp.arange(total_blocks, dtype=jnp.int32)[None, :]).astype(
        jnp.int32
    )
    before = jnp.cumsum(onehot, axis=0) - onehot
    ranking = jnp.sum(before * onehot, axis=1)
    return pair_blocks * capacity + ranking


def pick_columns(values, offsets):
    lanes = jnp.arange(BLK, dtype=jnp.int32)
    hit = offsets[:, :, None] == lanes[None, None, :]
    return jnp.sum(jnp.where(hit, values[:, None, :], 0.0), axis=2)


def spread_columns(picked, offsets):
    lanes = jnp.arange(BLK, dtype=jnp.int32)[None, :]
    out = jnp.zeros((picked.shape[0], BLK), picked.dtype)
    for j in range(PER):
        out = jnp.where(offsets[:, j : j + 1] == lanes, picked[:, j : j + 1], out)
    return out


def per_device(
    activations, center_bias, encoder_weight, encoder_bias, decoder_weight, row_blocks, pick_offsets
):
    group_rows, feature_width = activations.shape
    owners = lax.axis_size("lat")
    owned_blocks = encoder_bias.shape[0] // BLK
    total_blocks = owned_blocks * owners
    capacity = 2 * group_rows * KB // total_blocks
    slot_count = total_blocks * capacity
    per_owner = owned_blocks * capacity
    target = slot_targets(row_blocks, total_blocks, capacity)
    slots = jnp.arange(slot_count, dtype=jnp.int32)
    pair_hot = target[None, :] == slots[:, None]
    row_hot = jnp.any(pair_hot.reshape(slot_count, group_rows, KB), axis=2).astype(jnp.bfloat16)
    pair_hot = pair_hot.astype(jnp.bfloat16)
    centered = (activations - center_bias[None, :]).astype(jnp.bfloat16)
    outgoing = jnp.dot(row_hot, centered, preferred_element_type=jnp.float32).astype(jnp.bfloat16)
    offs_plus = (pick_offsets.reshape(-1, PER) + 1).astype(jnp.bfloat16)
    out_offs = jnp.dot(pair_hot, offs_plus, preferred_element_type=jnp.float32).astype(jnp.int32)
    got_offs = lax.all_to_all(
        out_offs.reshape(owners, per_owner, PER), "lat", split_axis=0, concat_axis=0, tiled=True
    )
    got_rows = lax.all_to_all(
        outgoing.reshape(owners, per_owner, feature_width),
        "lat",
        split_axis=0,
        concat_axis=0,
        tiled=True,
    )
    got_rows = got_rows.reshape(slot_count, feature_width)
    offs = got_offs.reshape(slot_count, PER) - 1
    slot_block = slots // capacity % owned_blocks
    col_block = jnp.arange(owned_blocks * BLK, dtype=jnp.int32) // BLK
    own_col = slot_block[:, None] == col_block[None, :]

    def own_half(full):
        parts = full.reshape(slot_count, owned_blocks, BLK)
        sel = slot_block[:, None, None] == jnp.arange(owned_blocks, dtype=jnp.int32)[None, :, None]
        return jnp.sum(jnp.where(sel, parts, 0.0), axis=1)

    def widen(narrow):
        tiled = jnp.tile(narrow, (1, owned_blocks))
        return jnp.where(own_col, tiled, jnp.zeros_like(tiled))

    partial_full = jnp.dot(got_rows, encoder_weight, preferred_element_type=jnp.float32)
    partial = pick_columns(own_half(partial_full), offs)
    summed = lax.psum(partial, "row")
    bias_rows = own_half(jnp.broadcast_to(encoder_bias[None, :], (slot_count, owned_blocks * BLK)))
    pre_picked = summed + pick_columns(bias_rows, offs)
    latent = spread_columns(pre_picked, offs).astype(jnp.bfloat16)
    latent_wide = widen(latent)
    decoded = jnp.dot(latent_wide, decoder_weight, preferred_element_type=jnp.float32).astype(
        jnp.bfloat16
    )
    returned = lax.all_to_all(
        decoded.reshape(owners, per_owner, feature_width),
        "lat",
        split_axis=0,
        concat_axis=0,
        tiled=True,
    ).reshape(slot_count, feature_width)
    rebuilt = lax.dot_general(
        row_hot, returned, (((0,), (0,)), ((), ())), preferred_element_type=jnp.float32
    )
    recon_error = center_bias[None, :] + rebuilt - activations
    loss_part = jnp.sum(recon_error * recon_error, axis=1)
    error_b = recon_error.astype(jnp.bfloat16)
    out_error = jnp.dot(row_hot, error_b, preferred_element_type=jnp.float32).astype(jnp.bfloat16)
    got_error = lax.all_to_all(
        out_error.reshape(owners, per_owner, feature_width),
        "lat",
        split_axis=0,
        concat_axis=0,
        tiled=True,
    ).reshape(slot_count, feature_width)
    decoder_grad = lax.dot_general(
        latent_wide, got_error, (((0,), (0,)), ((), ())), preferred_element_type=jnp.float32
    ).astype(jnp.bfloat16)
    dlatent_full = lax.dot_general(
        got_error, decoder_weight, (((1,), (1,)), ((), ())), preferred_element_type=jnp.float32
    )
    dlatent_part = pick_columns(own_half(dlatent_full), offs)
    dlatent, loss_total = lax.psum((dlatent_part, loss_part), "row")
    grad_pre = spread_columns(dlatent, offs).astype(jnp.bfloat16)
    grad_wide = widen(grad_pre)
    encoder_grad = lax.dot_general(
        got_rows, grad_wide, (((0,), (0,)), ((), ())), preferred_element_type=jnp.float32
    ).astype(jnp.bfloat16)
    bias_grad = jnp.sum(grad_wide.astype(jnp.float32), axis=0)
    row_loss = loss_total / D
    return (encoder_grad, decoder_grad, bias_grad, row_loss)


def solution(mesh):
    return jax.shard_map(
        per_device,
        mesh=mesh,
        in_specs=(
            P("lat", "row"),
            P("row"),
            P("row", "lat"),
            P("lat"),
            P("lat", "row"),
            P("lat", None),
            P("lat", None, None),
        ),
        out_specs=(P("row", "lat"), P("lat", "row"), P("lat"), P("lat")),
        check_vma=False,
    )
```

profile of v0, /device:TPU:4, one launch (start us, length us, event | category | flops | bytes accessed | tf_op | source)
XLA Modules:
  0.0 398.2 jit_solution(482381687215918004)
XLA Ops:
  4.9 10.6 %all-to-all-start.1 = ((s32[64,1,192]{2,1,0:T(1,128)}), s32[64,1,192]{2,1,0:T(1,128)S(1)}, u32[]{:S(2)}, u32[]{:S(2)}) async-start(s32[64,1,192]{2,1,0:T(1,128)} %reshape.842), calls=%async_computation.1 | async-start | bytes 131072 | tf_op jit(solution)/shard_map/all_to_all | solution.py:55
  16.8 2.8 convolution_convert_fusion.2
  19.6 4.1 %all-to-all-done.1 = s32[64,1,192]{2,1,0:T(1,128)S(1)} async-done(((s32[64,1,192]{2,1,0:T(1,128)}), s32[64,1,192]{2,1,0:T(1,128)S(1)}, u32[]{:S(2)}, u32[]{:S(2)}) %all-to-all-start.1) | async-done | bytes 49184 | tf_op jit(solution)/shard_map/all_to_all | solution.py:55
  23.7 7.4 %all-to-all-start = ((bf16[64,24,1024]{2,1,0:T(8,128)(2,1)}), bf16[64,24,1024]{2,1,0:T(8,128)(2,1)}, u32[]{:S(2)}, u32[]{:S(2)}) async-start(bf16[64,24,1024]{2,1,0:T(8,128)(2,1)} %bitcast.63), calls=%async_computation | async-start | bytes 6291456 | tf_op jit(solution)/shard_map/all_to_all | solution.py:58
  34.4 70.5 %all-to-all-done = bf16[64,24,1024]{2,1,0:T(8,128)(2,1)} async-done(((bf16[64,24,1024]{2,1,0:T(8,128)(2,1)}), bf16[64,24,1024]{2,1,0:T(8,128)(2,1)}, u32[]{:S(2)}, u32[]{:S(2)}) %all-to-all-start) | async-done | bytes 3145760 | tf_op jit(solution)/shard_map/all_to_all | solution.py:58
  104.9 4.0 %fusion.4 = f32[1536,128]{1,0:T(8,128)S(1)} fusion(bf16[1536,1024,1]{1,0,2:T(8,128)(2,1)} %bitcast.6, bf16[2,128,1024]{2,1,0:T(8,128)(2,1)S(1)} %bitcast.73, pred[1536,2]{0,1:T(4,128)(4,1)S(1)} %iota_compare_fusion.17), kind=kOutput, calls=%fused_computation.21 | convolution fusion | flops 805896192 | bytes 4459520 | tf_op jit(solution)/shard_map/dot_general | solution.py:80
  108.9 8.5 %select_reduce_fusion.1 = (f32[1536,8]{1,0:T(8,128)}, f32[1536,8]{1,0:T(8,128)S(1)}) fusion(f32[1536,128]{1,0:T(8,128)S(1)} %select_reduce_fusion.3, s32[1536,8]{1,0:T(8,128)S(1)} %copy.55, f32[1536,128]{1,0:T(8,128)S(1)} %fusion.4), kind=kLoop, calls=%fused_computation.1 | loop fusion | flops 7839744 | bytes 1720320 | tf_op jit(solution)/shard_map/reduce_sum | solution.py:25
  117.3 42.3 %psum.21 = f32[1536,8]{1,0:T(8,128)S(1)} all-reduce(f32[1536,8]{1,0:T(8,128)S(1)} %get-tuple-element.21), channel_id=1, replica_groups=mesh['lat'=64,'row'=8] {'row'}, use_global_device_ids=true, to_apply=%region_6.7 | all-reduce | flops 12288 | bytes 98304 | tf_op jit(solution)/shard_map/psum | solution.py:82
  159.6 1.2 add.87
  160.8 3.1 slice_reduce_fusion.15
  163.9 3.8 select_convert_fusion.1
  168.2 1.0 convolution_convert_fusion.1
  169.2 80.9 %all_to_all.20 = bf16[64,24,1024]{2,1,0:T(8,128)(2,1)S(1)} all-to-all(bf16[64,24,1024]{2,1,0:T(8,128)(2,1)S(1)} %bitcast.66), channel_id=1, replica_groups=mesh['lat'=64,'row'=8] {'lat'}, dimensions={0} | all-to-all | bytes 6291456 | tf_op jit(solution)/shard_map/all_to_all | solution.py:90
  251.1 2.8 convolution_convert_fusion
  253.9 5.8 %all-to-all-start.3 = ((bf16[64,24,1024]{2,1,0:T(8,128)(2,1)}), bf16[64,24,1024]{2,1,0:T(8,128)(2,1)}, u32[]{:S(2)}, u32[]{:S(2)}) async-start(bf16[64,24,1024]{2,1,0:T(8,128)(2,1)} %bitcast.64), calls=%async_computation.3 | async-start | bytes 6291456 | tf_op jit(solution)/shard_map/all_to_all | solution.py:104
  259.7 73.6 %all-to-all-done.3 = bf16[64,24,1024]{2,1,0:T(8,128)(2,1)} async-done(((bf16[64,24,1024]{2,1,0:T(8,128)(2,1)}), bf16[64,24,1024]{2,1,0:T(8,128)(2,1)}, u32[]{:S(2)}, u32[]{:S(2)}) %all-to-all-start.3) | async-done | bytes 3145760 | tf_op jit(solution)/shard_map/all_to_all | solution.py:104
  333.4 4.0 fusion.5
  337.4 4.8 %select_reduce_fusion = f32[1536,8]{1,0:T(8,128)S(1)} fusion(f32[1536,128]{1,0:T(8,128)S(1)} %fusion.5, s32[1536,8]{1,0:T(8,128)S(1)} %copy.55), kind=kLoop, calls=%fused_computation | loop fusion | flops 4706304 | bytes 884736 | tf_op jit(solution)/shard_map/reduce_sum | solution.py:25
  342.2 35.4 %all-reduce = (f32[1536,8]{1,0:T(8,128)S(1)}, f32[192]{0:T(256)S(1)}) all-reduce(f32[1536,8]{1,0:T(8,128)S(1)} %select_reduce_fusion, f32[192]{0:T(256)S(1)} %get-tuple-element.34), channel_id=1, replica_groups=mesh['lat'=64,'row'=8] {'row'}, use_global_device_ids=true, to_apply=%region_11.12 | all-reduce | flops 12480 | bytes 99840 | tf_op jit(solution)/shard_map/psum | solution.py:118
  377.6 3.1 slice_reduce_fusion.7
  380.8 3.8 select_convert_fusion
  384.6 4.8 %compare_select_fusion = (bf16[1536,2,128]{2,1,0:T(2,128)(2,1)S(1)}, bf16[1536,2,128]{2,1,0:T(2,128)(2,1)S(1)}) fusion(s32[2,128]{1,0:T(2,128)S(1)} %and_select_fusion.1, s32[1536]{0:T(1024)S(1)} %add_select_fusion, bf16[1536,128]{1,0:T(8,128)(2,1)S(1)} %select_convert_fusion.1, bf16[1536,128]{1,0:T(8,128)(2,1)S(1)} %select_convert_fusion), kind=kLoop, calls=%fused_computation.11 | loop fusion | flops 1179648 | bytes 2366464 | tf_op jit(solution)/shard_map/jit(_where)/select_n | solution.py:78
  390.7 3.7 convolution_convert_fusion.3
  394.4 3.7 convolution_convert_fusion.4
  (56 shorter events, 11.3 us)
Async XLA Ops:
  0.6 167.6 %copy-start = (bf16[256,1024]{1,0:T(8,128)(2,1)S(1)}, bf16[256,1024]{1,0:T(8,128)(2,1)}, u32[]{:S(2)}) copy-start(bf16[256,1024]{1,0:T(8,128)(2,1)} %param.11) | copy-start | bytes 1572868
  0.6 1.9 copy-start.4
  1.5 14.2 %copy-start.5 = (s32[192,4]{0,1:T(4,128)S(1)}, s32[192,4]{0,1:T(4,128)}, u32[]{:S(2)}) copy-start(s32[192,4]{0,1:T(4,128)} %param.12) | copy-start | bytes 9220
  1.9 14.9 %copy-start.1 = (f32[192,1024]{1,0:T(8,128)S(1)}, f32[192,1024]{1,0:T(8,128)}, u32[]{:S(2)}) copy-start(f32[192,1024]{1,0:T(8,128)} %param.7) | copy-start | bytes 2359300
  1.9 14.9 %copy-start.6 = (f32[1024]{0:T(1024)S(1)}, f32[1024]{0:T(1024)}, u32[]{:S(2)}) copy-start(f32[1024]{0:T(1024)} %param.8) | copy-start | bytes 12292
  4.9 18.8 %all-to-all-start.1 = ((s32[64,1,192]{2,1,0:T(1,128)}), s32[64,1,192]{2,1,0:T(1,128)S(1)}, u32[]{:S(2)}, u32[]{:S(2)}) async-start(s32[64,1,192]{2,1,0:T(1,128)} %reshape.842), calls=%async_computation.1 | async-start | bytes 131072 | tf_op jit(solution)/shard_map/all_to_all | solution.py:55
  23.7 7.4 %copy-start.3 = (bf16[1024,256]{1,0:T(8,128)(2,1)S(1)}, bf16[1024,256]{1,0:T(8,128)(2,1)}, u32[]{:S(2)}) copy-start(bf16[1024,256]{1,0:T(8,128)(2,1)} %param.9) | copy-start | bytes 1572868
  23.7 7.7 %copy-start.7 = (f32[256]{0:T(256)S(1)}, f32[256]{0:T(256)}, u32[]{:S(2)}) copy-start(f32[256]{0:T(256)} %param.10) | copy-start | bytes 3076
  23.7 81.2 %all-to-all-start = ((bf16[64,24,1024]{2,1,0:T(8,128)(2,1)}), bf16[64,24,1024]{2,1,0:T(8,128)(2,1)}, u32[]{:S(2)}, u32[]{:S(2)}) async-start(bf16[64,24,1024]{2,1,0:T(8,128)(2,1)} %bitcast.63), calls=%async_computation | async-start | bytes 6291456 | tf_op jit(solution)/shard_map/all_to_all | solution.py:58
  169.2 80.9 %copy-start.2 = (f32[192,1024]{1,0:T(8,128)S(1)}, f32[192,1024]{1,0:T(8,128)}, u32[]{:S(2)}) copy-start(f32[192,1024]{1,0:T(8,128)} %param.7) | copy-start | bytes 2359300
  253.9 79.5 %all-to-all-start.3 = ((bf16[64,24,1024]{2,1,0:T(8,128)(2,1)}), bf16[64,24,1024]{2,1,0:T(8,128)(2,1)}, u32[]{:S(2)}, u32[]{:S(2)}) async-start(bf16[64,24,1024]{2,1,0:T(8,128)(2,1)} %bitcast.64), calls=%async_computation.3 | async-start | bytes 6291456 | tf_op jit(solution)/shard_map/all_to_all | solution.py:104
where the time goes:
time: 399 us; the launch traced here: 398 us
  blocking collectives  159 us (40%)
  waiting for transfers between devices  148 us (37%)
  other arithmetic  31.3 us (8%)
  matrix products  23.9 us (6%)
  starting transfers between devices  23.8 us (6%)
  local copies, waits for them, and re-layouts  11.3 us (3%)
    all_to_all x1, blocking collectives, per_device(): lax.all_to_all(decoded.reshape(owners, per_owner, feature_width), 'lat',...  80.9 us
    all_to_all x1, waiting for transfers between devices, per_device(): lax.all_to_all(out_error.reshape(owners, per_owner, feature_width), 'lat'...  73.6 us
    all_to_all x1, waiting for transfers between devices, per_device(): lax.all_to_all(outgoing.reshape(owners, per_owner, feature_width), 'lat',...  70.5 us
    psum x1, blocking collectives, per_device(): summed = lax.psum(partial, 'row')  42.3 us
    psum x1, blocking collectives, per_device(): dlatent, loss_total = lax.psum((dlatent_part, loss_part), 'row')  35.4 us
    reduce_sum x2, other arithmetic, pick_columns(): return jnp.sum(jnp.where(hit, values[:, None, :], 0.0), axis=2)  13.3 us
    all_to_all x1, starting transfers between devices, per_device(): lax.all_to_all(out_offs.reshape(owners, per_owner, PER), 'lat', split_axi...  10.6 us
  transfers between devices with their start and end apart: 3, of which 3 were waited for; matrix products, arithmetic and copies ran while one was open for 2% of the time, Pallas kernels for 0%

commit v1 on v0

--- a/solution.py
+++ b/solution.py
@@ -1,3 +1,4 @@
+import functools
 import jax
 import jax.numpy as jnp
 from jax import lax
@@ -7,6 +8,14 @@
 BLK = 128
 KB = 4
 PER = 8
+
+
+def mix_the_tables(block_here, across):
+    res = lax.all_gather(block_here, across)
+    return jnp.sum(res, axis=0)
+
+
+try_all_the_space = functools.partial(mix_the_tables, across="row")
 
 
 def slot_targets(row_blocks, total_blocks, capacity):
@@ -79,7 +88,7 @@
 
     partial_full = jnp.dot(got_rows, encoder_weight, preferred_element_type=jnp.float32)
     partial = pick_columns(own_half(partial_full), offs)
-    summed = lax.psum(partial, "row")
+    summed = try_all_the_space(partial)
     bias_rows = own_half(jnp.broadcast_to(encoder_bias[None, :], (slot_count, owned_blocks * BLK)))
     pre_picked = summed + pick_columns(bias_rows, offs)
     latent = spread_columns(pre_picked, offs).astype(jnp.bfloat16)

time: 399 us -> 427 us (1.070)
  the two profiles are of different devices: /device:TPU:4 before, /device:TPU:8 now
where the time goes in v1:
time: 427 us
  blocking collectives  187 us (44%)
  waiting for transfers between devices  147 us (34%)
  other arithmetic  34.1 us (8%)
  matrix products  23.9 us (6%)
  starting transfers between devices  23.8 us (6%)
  local copies, waits for them, and re-layouts  9.84 us (2%)
    all_to_all x1, blocking collectives, per_device(): lax.all_to_all(decoded.reshape(owners, per_owner, feature_width), 'lat',...  79.1 us
    all_to_all x1, waiting for transfers between devices, per_device(): lax.all_to_all(out_error.reshape(owners, per_owner, feature_width), 'lat'...  72.8 us
    all_gather x1, blocking collectives, mix_the_tables(): res = lax.all_gather(block_here, across)  69.9 us
    all_to_all x1, waiting for transfers between devices, per_device(): lax.all_to_all(outgoing.reshape(owners, per_owner, feature_width), 'lat',...  69.6 us
    psum x1, blocking collectives, per_device(): dlatent, loss_total = lax.psum((dlatent_part, loss_part), 'row')  37.6 us
    reduce_sum x2, other arithmetic, pick_columns(): return jnp.sum(jnp.where(hit, values[:, None, :], 0.0), axis=2)  13.3 us
    all_to_all x1, starting transfers between devices, per_device(): lax.all_to_all(out_offs.reshape(owners, per_owner, PER), 'lat', split_axi...  10.6 us
  transfers between devices with their start and end apart: 3, of which 3 were waited for; matrix products, arithmetic and copies ran while one was open for 2% of the time, Pallas kernels for 0%

profile of v1, /device:TPU:8, one launch (start us, length us, event | category | flops | bytes accessed | tf_op | source)
XLA Modules:
  0.0 426.6 jit_solution(4217086036829463737)
XLA Ops:
  5.6 10.6 %all-to-all-start.1 = ((s32[64,1,192]{2,1,0:T(1,128)}), s32[64,1,192]{2,1,0:T(1,128)S(1)}, u32[]{:S(2)}, u32[]{:S(2)}) async-start(s32[64,1,192]{2,1,0:T(1,128)} %reshape.843), calls=%async_computation.1 | async-start | bytes 131072 | tf_op jit(solution)/shard_map/all_to_all | solution.py:64
  17.4 2.8 convolution_convert_fusion.2
  20.2 5.1 %all-to-all-done.1 = s32[64,1,192]{2,1,0:T(1,128)S(1)} async-done(((s32[64,1,192]{2,1,0:T(1,128)}), s32[64,1,192]{2,1,0:T(1,128)S(1)}, u32[]{:S(2)}, u32[]{:S(2)}) %all-to-all-start.1) | async-done | bytes 49184 | tf_op jit(solution)/shard_map/all_to_all | solution.py:64
  25.3 6.5 %all-to-all-start = ((bf16[64,24,1024]{2,1,0:T(8,128)(2,1)}), bf16[64,24,1024]{2,1,0:T(8,128)(2,1)}, u32[]{:S(2)}, u32[]{:S(2)}) async-start(bf16[64,24,1024]{2,1,0:T(8,128)(2,1)} %bitcast.65), calls=%async_computation | async-start | bytes 6291456 | tf_op jit(solution)/shard_map/all_to_all | solution.py:67
  35.1 69.6 %all-to-all-done = bf16[64,24,1024]{2,1,0:T(8,128)(2,1)} async-done(((bf16[64,24,1024]{2,1,0:T(8,128)(2,1)}), bf16[64,24,1024]{2,1,0:T(8,128)(2,1)}, u32[]{:S(2)}, u32[]{:S(2)}) %all-to-all-start) | async-done | bytes 3145760 | tf_op jit(solution)/shard_map/all_to_all | solution.py:67
  104.7 4.0 fusion.4
  108.7 8.4 %select_reduce_fusion.1 = (f32[1536,8]{1,0:T(8,128)}, f32[1536,8]{1,0:T(8,128)S(1)}) fusion(f32[1536,128]{1,0:T(8,128)S(1)} %select_reduce_fusion.3, s32[1536,8]{1,0:T(8,128)S(1)} %copy.57, f32[1536,128]{1,0:T(8,128)S(1)} %fusion.4), kind=kLoop, calls=%fused_computation.1 | loop fusion | flops 7839744 | bytes 1720320 | tf_op jit(solution)/shard_map/reduce_sum | solution.py:34
  117.1 1.4 copy.60
  118.5 69.9 %all-gather = f32[12288,8]{1,0:T(8,128)} all-gather(f32[1536,8]{1,0:T(8,128)S(1)} %get-tuple-element.13), channel_id=2, replica_groups=mesh['lat'=64,'row'=8] {'row'}, dimensions={0}, use_global_device_ids=true | all-gather | bytes 442368 | tf_op jit(solution)/shard_map/all_gather | solution.py:14
  188.4 3.3 reduce_sum.98
  192.1 3.8 select_convert_fusion.1
  196.3 1.0 convolution_convert_fusion.1
  197.4 79.1 %all_to_all.20 = bf16[64,24,1024]{2,1,0:T(8,128)(2,1)S(1)} all-to-all(bf16[64,24,1024]{2,1,0:T(8,128)(2,1)S(1)} %bitcast.68), channel_id=1, replica_groups=mesh['lat'=64,'row'=8] {'lat'}, dimensions={0} | all-to-all | bytes 6291456 | tf_op jit(solution)/shard_map/all_to_all | solution.py:99
  277.4 2.8 convolution_convert_fusion
  280.2 6.7 %all-to-all-start.3 = ((bf16[64,24,1024]{2,1,0:T(8,128)(2,1)}), bf16[64,24,1024]{2,1,0:T(8,128)(2,1)}, u32[]{:S(2)}, u32[]{:S(2)}) async-start(bf16[64,24,1024]{2,1,0:T(8,128)(2,1)} %bitcast.66), calls=%async_computation.3 | async-start | bytes 6291456 | tf_op jit(solution)/shard_map/all_to_all | solution.py:113
  286.9 72.8 %all-to-all-done.3 = bf16[64,24,1024]{2,1,0:T(8,128)(2,1)} async-done(((bf16[64,24,1024]{2,1,0:T(8,128)(2,1)}), bf16[64,24,1024]{2,1,0:T(8,128)(2,1)}, u32[]{:S(2)}, u32[]{:S(2)}) %all-to-all-start.3) | async-done | bytes 3145760 | tf_op jit(solution)/shard_map/all_to_all | solution.py:113
  359.7 4.0 fusion.5
  363.7 4.8 %select_reduce_fusion = f32[1536,8]{1,0:T(8,128)S(1)} fusion(f32[1536,128]{1,0:T(8,128)S(1)} %fusion.5, s32[1536,8]{1,0:T(8,128)S(1)} %copy.57), kind=kLoop, calls=%fused_computation | loop fusion | flops 4706304 | bytes 884736 | tf_op jit(solution)/shard_map/reduce_sum | solution.py:34
  368.5 37.6 %all-reduce = (f32[1536,8]{1,0:T(8,128)S(1)}, f32[192]{0:T(256)S(1)}) all-reduce(f32[1536,8]{1,0:T(8,128)S(1)} %select_reduce_fusion, f32[192]{0:T(256)S(1)} %get-tuple-element.34), channel_id=1, replica_groups=mesh['lat'=64,'row'=8] {'row'}, use_global_device_ids=true, to_apply=%region_11.12 | all-reduce | flops 12480 | bytes 99840 | tf_op jit(solution)/shard_map/psum | solution.py:127
  406.1 3.1 slice_reduce_fusion.7
  409.3 3.8 select_convert_fusion
  413.9 4.7 %compare_select_fusion = (bf16[1536,2,128]{2,1,0:T(2,128)(2,1)S(1)}, bf16[1536,2,128]{2,1,0:T(2,128)(2,1)S(1)}) fusion(s32[2,128]{1,0:T(2,128)S(1)} %and_select_fusion.1, s32[1536]{0:T(1024)S(1)} %add_select_fusion, bf16[1536,128]{1,0:T(8,128)(2,1)S(1)} %select_convert_fusion.1, bf16[1536,128]{1,0:T(8,128)(2,1)S(1)} %select_convert_fusion), kind=kLoop, calls=%fused_computation.11 | loop fusion | flops 1179648 | bytes 2366464 | tf_op jit(solution)/shard_map/jit(_where)/select_n | solution.py:87
  419.2 3.7 convolution_convert_fusion.3
  422.9 3.7 convolution_convert_fusion.4
  (57 shorter events, 12.5 us)
Async XLA Ops:
  0.6 195.7 %copy-start = (bf16[256,1024]{1,0:T(8,128)(2,1)S(1)}, bf16[256,1024]{1,0:T(8,128)(2,1)}, u32[]{:S(2)}) copy-start(bf16[256,1024]{1,0:T(8,128)(2,1)} %param.11) | copy-start | bytes 1572868
  1.5 14.9 %copy-start.4 = (s32[192,4]{0,1:T(4,128)S(1)}, s32[192,4]{0,1:T(4,128)}, u32[]{:S(2)}) copy-start(s32[192,4]{0,1:T(4,128)} %param.12) | copy-start | bytes 9220
  2.6 14.8 %copy-start.1 = (f32[192,1024]{1,0:T(8,128)S(1)}, f32[192,1024]{1,0:T(8,128)}, u32[]{:S(2)}) copy-start(f32[192,1024]{1,0:T(8,128)} %param.7) | copy-start | bytes 2359300
  2.6 14.8 %copy-start.5 = (f32[1024]{0:T(1024)S(1)}, f32[1024]{0:T(1024)}, u32[]{:S(2)}) copy-start(f32[1024]{0:T(1024)} %param.8) | copy-start | bytes 12292
  5.6 19.7 %all-to-all-start.1 = ((s32[64,1,192]{2,1,0:T(1,128)}), s32[64,1,192]{2,1,0:T(1,128)S(1)}, u32[]{:S(2)}, u32[]{:S(2)}) async-start(s32[64,1,192]{2,1,0:T(1,128)} %reshape.843), calls=%async_computation.1 | async-start | bytes 131072 | tf_op jit(solution)/shard_map/all_to_all | solution.py:64
  25.3 6.5 %copy-start.3 = (bf16[1024,256]{1,0:T(8,128)(2,1)S(1)}, bf16[1024,256]{1,0:T(8,128)(2,1)}, u32[]{:S(2)}) copy-start(bf16[1024,256]{1,0:T(8,128)(2,1)} %param.9) | copy-start | bytes 1572868
  25.3 6.8 %copy-start.6 = (f32[256]{0:T(256)S(1)}, f32[256]{0:T(256)}, u32[]{:S(2)}) copy-start(f32[256]{0:T(256)} %param.10) | copy-start | bytes 3076
  25.3 79.4 %all-to-all-start = ((bf16[64,24,1024]{2,1,0:T(8,128)(2,1)}), bf16[64,24,1024]{2,1,0:T(8,128)(2,1)}, u32[]{:S(2)}, u32[]{:S(2)}) async-start(bf16[64,24,1024]{2,1,0:T(8,128)(2,1)} %bitcast.65), calls=%async_computation | async-start | bytes 6291456 | tf_op jit(solution)/shard_map/all_to_all | solution.py:67
  197.4 79.1 %copy-start.2 = (f32[192,1024]{1,0:T(8,128)S(1)}, f32[192,1024]{1,0:T(8,128)}, u32[]{:S(2)}) copy-start(f32[192,1024]{1,0:T(8,128)} %param.7) | copy-start | bytes 2359300
  280.2 79.5 %all-to-all-start.3 = ((bf16[64,24,1024]{2,1,0:T(8,128)(2,1)}), bf16[64,24,1024]{2,1,0:T(8,128)(2,1)}, u32[]{:S(2)}, u32[]{:S(2)}) async-start(bf16[64,24,1024]{2,1,0:T(8,128)(2,1)} %bitcast.66), calls=%async_computation.3 | async-start | bytes 6291456 | tf_op jit(solution)/shard_map/all_to_all | solution.py:113
